TPU v7x, 256 devices: a whole 4x4x8 slice. The times are simulated.
256 devices in a mesh: req: 32 (over x, z), kv: 8 (over y, core).
Axes of the slice: x: 4, y: 4, z: 8, core: 2. Of those that a mesh axis runs over, the one named last changes fastest.
Arguments:
- states: bfloat16 [256, 2560], P(('req', 'kv')), may hold values from -6 to 6
- norm_gain: bfloat16 [2560], replicated, may hold values from 0.099609375 to 1.8984375
- w_query: bfloat16 [2560, 2560], P(None, 'kv'), may hold values from -0.125 to 0.125
- key_projection_weight: bfloat16 [2560, 640], P(None, 'kv'), may hold values from -0.125 to 0.125
- value_projection_weight: bfloat16 [2560, 640], P(None, 'kv'), may hold values from -0.125 to 0.125
- cache_keys: bfloat16 [256, 8, 80, 4096], P('req', 'kv')
- value_cache_slots: bfloat16 [256, 8, 80, 4096], P('req', 'kv'), may hold values from -6 to 6
- lengths: int32 [256], P('req'), may hold values from 1 to 16383, as said below
- write_pos: int32 [256], P('req'), may hold values from 0 to 4095, as said below
- dealing: int32 [256], replicated, may hold values from 0 to 255, each once
Outputs:
- context: bfloat16 [256, 2560], P(('req', 'kv'))
Inputs may be any that keep to these rules, and one draw needn't show every extreme that they name: `lengths`: largest value is reached by some request in every draw. write_pos equals lengths modulo 4096. `dealing`: A permutation of the requests.
All inputs are finite; a program needn't handle non-finite values.
Results may differ from a plain program's by a relative error of at most 0.022.
The roundings to bfloat16 on the way count: a program that leaves them out, or rounds other values in their place, can miss the bound.
Values may be sent and summed in bfloat16 or wider, within the bound.
No kernel may reach another device: no remote copies, remote signals or barrier semaphores. Data moves between devices by JAX's collectives and lax.ppermute only.
A program may use at most 64 MiB of HBM per device.

v0:
```python
import jax
import jax.numpy as jnp
from jax import lax
from jax.sharding import PartitionSpec as P

HEAD_DIMENSION = 80


def apply_rotary(tensor, positions):
    half_width = tensor.shape[-1] // 2
    frequency = 10000.0 ** (-(jnp.arange(half_width, dtype=jnp.float32) * 2.0 / tensor.shape[-1]))
    angles = positions.astype(jnp.float32)[:, None] * frequency[None, :]
    cosine = jnp.cos(angles)[:, None, :]
    sine_part = jnp.sin(angles)[:, None, :]
    front_half = tensor[..., :half_width]
    back_half = tensor[..., half_width:]
    return jnp.concatenate(
        [front_half * cosine - back_half * sine_part, back_half * cosine + front_half * sine_part],
        axis=-1,
    )


def local(
    states,
    norm_gain,
    w_query,
    key_projection_weight,
    value_projection_weight,
    cache_keys,
    value_cache_slots,
    lengths,
    write_pos,
    dealing,
):
    kv_count = lax.axis_size("kv")
    per_device = states.shape[0]
    group_rows = per_device * kv_count
    group_index = lax.axis_index("req")
    kv_index = lax.axis_index("kv")
    total_rows = dealing.shape[0]
    dealt_ids = lax.dynamic_slice_in_dim(dealing, group_index * group_rows, group_rows)
    all_rows = lax.all_gather(states, ("req", "kv"), axis=0, tiled=True)
    dealt_rows = jnp.take(all_rows, dealt_ids, axis=0)
    wide_rows = dealt_rows.astype(jnp.float32)
    inv_rms = lax.rsqrt(jnp.mean(wide_rows * wide_rows, axis=1, keepdims=True) + 1e-05)
    normalized_input = (wide_rows * inv_rms * norm_gain.astype(jnp.float32)[None, :]).astype(
        jnp.bfloat16
    )
    head_size = HEAD_DIMENSION
    heads_dev = key_projection_weight.shape[1] // head_size
    queries_per_group = w_query.shape[1] // key_projection_weight.shape[1]
    window_size = cache_keys.shape[3]
    query_vectors = jnp.dot(normalized_input, w_query, preferred_element_type=jnp.float32).reshape(
        group_rows, heads_dev * queries_per_group, head_size
    )
    query_vectors = (
        apply_rotary(query_vectors, lengths)
        .astype(jnp.bfloat16)
        .reshape(group_rows, heads_dev, queries_per_group, head_size)
    )
    fresh_key_rows = jnp.dot(
        normalized_input, key_projection_weight, preferred_element_type=jnp.float32
    ).reshape(group_rows, heads_dev, head_size)
    fresh_key_rows = apply_rotary(fresh_key_rows, lengths).astype(jnp.bfloat16)
    fresh_value_rows = (
        jnp.dot(normalized_input, value_projection_weight, preferred_element_type=jnp.float32)
        .astype(jnp.bfloat16)
        .reshape(group_rows, heads_dev, head_size)
    )
    score_scale = 1.0 / head_size**0.5
    scores = (
        jnp.einsum("rkgh,rkhw->rkgw", query_vectors, cache_keys, preferred_element_type=jnp.float32)
        * score_scale
    )
    own_score = (
        jnp.einsum(
            "rkgh,rkh->rkg", query_vectors, fresh_key_rows, preferred_element_type=jnp.float32
        )
        * score_scale
    )
    slot_ids = lax.broadcasted_iota(jnp.int32, (group_rows, 1, 1, window_size), 3)
    at_write = slot_ids == write_pos[:, None, None, None]
    scores = jnp.where(at_write, own_score[..., None], scores)
    scores = jnp.where(slot_ids <= lengths[:, None, None, None], scores, -jnp.inf)
    row_max = jnp.max(scores, axis=-1, keepdims=True)
    expd = jnp.exp(scores - row_max)
    softmax_weights = (expd / jnp.sum(expd, axis=-1, keepdims=True)).astype(jnp.bfloat16)
    stale_weights = jnp.where(at_write, jnp.zeros((), jnp.bfloat16), softmax_weights)
    fresh_weight = jnp.sum(
        jnp.where(at_write, softmax_weights, jnp.zeros((), jnp.bfloat16)).astype(jnp.float32),
        axis=-1,
    )
    mixed = jnp.einsum(
        "rkgw,rkhw->rkgh", stale_weights, value_cache_slots, preferred_element_type=jnp.float32
    )
    mixed = mixed + fresh_weight[..., None] * fresh_value_rows[:, :, None, :].astype(jnp.float32)
    attended = mixed.reshape(group_rows, heads_dev * queries_per_group * head_size).astype(
        jnp.bfloat16
    )
    inverse = jnp.zeros((total_rows,), jnp.int32).at[dealing].set(jnp.arange(total_rows))
    request_rows = lax.all_to_all(attended, "kv", split_axis=0, concat_axis=1, tiled=True)
    all_context = lax.all_gather(request_rows, ("req", "kv"), axis=0, tiled=True)
    own_ids = lax.dynamic_slice_in_dim(
        inverse, (group_index * kv_count + kv_index) * per_device, per_device
    )
    result = jnp.take(all_context, own_ids, axis=0)
    return result


def solution(mesh):
    in_specs = (
        P(("req", "kv"), None),
        P(),
        P(None, "kv"),
        P(None, "kv"),
        P(None, "kv"),
        P("req", "kv", None, None),
        P("req", "kv", None, None),
        P("req"),
        P("req"),
        P(),
    )
    out_specs = P(("req", "kv"), None)
    return jax.shard_map(local, mesh=mesh, in_specs=in_specs, out_specs=out_specs, check_vma=False)
```

profile of v0, /device:TPU:1, one launch (start us, length us, event | category | flops | bytes accessed | tf_op | source)
XLA Modules:
  0.0 256.5 jit_solution(114267257454325564)
XLA Ops:
  6.5 0.7 all-gather.5.cloned.1.call-update
  7.3 0.7 convert_element_type.52
  8.0 0.7 convert_element_type.50
  8.7 0.8 compare_and_fusion
  9.6 0.8 iota_compare_fusion
  10.3 109.8 %all-gather.5.cloned.1.call-done = bf16[256,1,2560]{2,1,0:T(2,128)(2,1)} async-done(((bf16[1,1,2560]{2,1,0:T(2,128)(2,1)}), bf16[256,1,2560]{2,1,0:T(2,128)(2,1)}) %all-gather.5.cloned.1.call-update) | async-done | bytes 1310736 | tf_op jit(solution)/shard_map/all_gather | solution.py:42
  120.1 1.9 copy.19
  122.0 0.6 gather_fusion
  122.6 0.2 fusion.26
  122.8 1.3 convolution_bitcast_fusion
  124.2 1.3 fusion.22
  125.5 0.5 fusion.47
  126.3 0.2 fusion.38
  126.5 3.7 %fusion.49 = (f32[8,4]{1,0:T(8,128)S(1)}, f32[8,4,4096]{2,1,0:T(4,128)S(1)}) fusion(bf16[8,1,80,4096]{3,2,1,0:T(8,128)(2,1)} %param.15, f32[8,4]{1,0:T(8,128)S(1)} %broadcast_multiply_fusion, pred[8,4096]{1,0:T(8,128)(4,1)S(1)} %get-tuple-element.28, pred[8,4096]{1,0:T(8,128)(4,1)S(1)} %get-tuple-element.29, bf16[8,4,40]{2,1,0:T(4,128)(2,1)S(1)} %get-tuple-element.21, ...), kind=kOutput, calls=%fused_computation.64 | convolution fusion | flops 21641216 | bytes 5838080 | tf_op jit(solution)/shard_map/sub | solution.py:86
  130.2 0.4 convert_reduce_fusion
  130.5 3.9 %fusion.19 = bf16[8,4,80]{2,1,0:T(4,128)(2,1)S(1)} fusion(bf16[8,1,80,4096]{3,2,1,0:T(8,128)(2,1)} %param.16, bf16[8,4,4096]{2,1,0:T(4,128)(2,1)S(1)} %get-tuple-element.17, pred[8,4096]{1,0:T(8,128)(4,1)S(1)} %get-tuple-element.29, f32[8,80]{1,0:T(8,128)S(1)} %fusion.22, f32[8,4]{1,0:T(8,128)S(1)} %get-tuple-element.16), kind=kOutput, calls=%fused_computation.14 | convolution fusion | flops 21110272 | bytes 5545600 | tf_op jit(solution)/shard_map/rkgw,rkhw->rkgh/dot_general | solution.py:93
  134.6 0.5 broadcast.209
  135.1 0.7 reduce.7
  135.9 8.8 %all_to_all.13 = bf16[8,2,160]{2,1,0:T(2,128)(2,1)S(1)} all-to-all(bf16[8,2,160]{2,1,0:T(2,128)(2,1)S(1)} %reshape.323), channel_id=1, replica_groups=mesh['req'=32,'kv'=8] {'kv'}, dimensions={0} | all-to-all | bytes 10240 | tf_op jit(solution)/shard_map/all_to_all | solution.py:101
  144.9 0.7 reshape.311
  145.6 1.4 scatter_custom_fusion
  147.0 0.7 dynamic_slice.6
  149.6 98.7 %all-gather.7.cloned.1.call-done = bf16[256,1,2560]{2,1,0:T(2,128)(2,1)} async-done(((bf16[1,1,2560]{2,1,0:T(2,128)(2,1)}), bf16[256,1,2560]{2,1,0:T(2,128)(2,1)}) %all-gather.7.cloned.1.call-update) | async-done | bytes 1310736 | tf_op jit(solution)/shard_map/all_gather | solution.py:102
  248.3 1.3 fusion.29
  (22 shorter events, 0.9 us)
Async XLA Ops:
  6.5 119.0 %copy-start = (bf16[2560,320]{0,1:T(8,128)(2,1)S(1)}, bf16[2560,320]{0,1:T(8,128)(2,1)}, u32[]{:S(2)}) copy-start(bf16[2560,320]{0,1:T(8,128)(2,1)} %param.12) | copy-start | bytes 4915204
  6.5 113.6 %all-gather.5.cloned.1.call-start = ((), (), s32[]{:S(2)}) async-start(), calls=%async_computation.1 | async-start | bytes 2631680 | tf_op jit(solution)/shard_map/all_gather | solution.py:42
  7.3 241.1 %all-gather.7.cloned.1.call-start = ((), (), s32[]{:S(2)}) async-start(), calls=%async_computation.2 | async-start | bytes 2631680 | tf_op jit(solution)/shard_map/all_gather | solution.py:102
  126.5 19.1 %copy-start.1 = (s32[256]{0:T(256)S(1)}, s32[256]{0:T(256)}, u32[]{:S(2)}) copy-start(s32[256]{0:T(256)} %param.19) | copy-start | bytes 3076
Sparse Core Ops, SparseCore 0:
  11.0 109.0 all-gather.4
  145.7 102.5 all-gather.6
where the time goes:
time: 257 us; the launch traced here: 256 us
  waiting for transfers between devices  209 us (81%)
  between operations  15.4 us (6%)
  matrix products  10.9 us (4%)
  blocking collectives  8.83 us (3%)
  local copies, waits for them, and re-layouts  6.11 us (2%)
  other arithmetic  5.97 us (2%)
    all_gather x1, waiting for transfers between devices, local(): all_rows = lax.all_gather(states, ('req', 'kv'), axis=0, tiled=True)  110 us
    all_gather x1, waiting for transfers between devices, local(): lax.all_gather(request_rows, ('req', 'kv'), axis=0, tiled=True)  98.7 us
    all_to_all x1, blocking collectives, local(): lax.all_to_all(attended, 'kv', split_axis=0, concat_axis=1, tiled=True)  8.83 us
  transfers between devices with their start and end apart: 2, of which 2 were waited for; matrix products, arithmetic and copies ran while one was open for 2% of the time, Pallas kernels for 0%

commit v1 on v0

--- a/solution.py
+++ b/solution.py
@@ -98,7 +98,10 @@
         jnp.bfloat16
     )
     inverse = jnp.zeros((total_rows,), jnp.int32).at[dealing].set(jnp.arange(total_rows))
-    request_rows = lax.all_to_all(attended, "kv", split_axis=0, concat_axis=1, tiled=True)
+    request_rows = jnp.concatenate(
+        lax.all_to_all(jnp.stack(jnp.split(attended, lax.axis_size("kv"), axis=0)), "kv", 0, 0),
+        axis=1,
+    )
     all_context = lax.all_gather(request_rows, ("req", "kv"), axis=0, tiled=True)
     own_ids = lax.dynamic_slice_in_dim(
         inverse, (group_index * kv_count + kv_index) * per_device, per_device

time: 257 us -> 258 us (level)
  no operation moved by 1% of the time
where the time goes in v1:
time: 258 us; the launch traced here: 257 us
  waiting for transfers between devices  209 us (81%)
  between operations  15.4 us (6%)
  matrix products  10.9 us (4%)
  blocking collectives  8.83 us (3%)
  local copies, waits for them, and re-layouts  6.79 us (3%)
  other arithmetic  5.97 us (2%)
    all_gather x1, waiting for transfers between devices, local(): all_rows = lax.all_gather(states, ('req', 'kv'), axis=0, tiled=True)  110 us
    all_gather x1, waiting for transfers between devices, local(): lax.all_gather(request_rows, ('req', 'kv'), axis=0, tiled=True)  98.7 us
    all_to_all x1, blocking collectives, local(): lax.all_to_all(jnp.stack(jnp.split(attended, lax.axis_size('kv'), axis=0)...  8.83 us
  transfers between devices with their start and end apart: 2, of which 2 were waited for; matrix products, arithmetic and copies ran while one was open for 2% of the time, Pallas kernels for 0%

profile of v1, /device:TPU:1, one launch (start us, length us, event | category | flops | bytes accessed | tf_op | source)
XLA Modules:
  0.0 257.2 jit_solution(3858385671227756299)
XLA Ops:
  6.5 0.7 all-gather.5.cloned.1.call-update
  7.3 0.7 convert_element_type.43
  8.0 0.7 convert_element_type.41
  8.7 0.8 compare_and_fusion
  9.6 0.8 iota_compare_fusion
  10.3 109.8 %all-gather.5.cloned.1.call-done = bf16[256,1,2560]{2,1,0:T(2,128)(2,1)} async-done(((bf16[1,1,2560]{2,1,0:T(2,128)(2,1)}), bf16[256,1,2560]{2,1,0:T(2,128)(2,1)}) %all-gather.5.cloned.1.call-update) | async-done | bytes 1310736 | tf_op jit(solution)/shard_map/all_gather | solution.py:42
  120.1 1.9 copy.25
  122.0 0.6 gather_fusion
  122.6 0.2 fusion.26
  122.8 1.3 convolution_bitcast_fusion
  124.2 1.3 fusion.22
  125.5 0.5 fusion.47
  126.3 0.2 fusion.38
  126.5 3.7 %fusion.50 = (f32[8,4]{1,0:T(8,128)S(1)}, f32[8,4,4096]{2,1,0:T(4,128)S(1)}) fusion(bf16[8,1,80,4096]{3,2,1,0:T(8,128)(2,1)} %param.15, f32[8,4]{1,0:T(8,128)S(1)} %broadcast_multiply_fusion, pred[8,4096]{1,0:T(8,128)(4,1)S(1)} %get-tuple-element.36, pred[8,4096]{1,0:T(8,128)(4,1)S(1)} %get-tuple-element.37, bf16[8,4,40]{2,1,0:T(4,128)(2,1)S(1)} %get-tuple-element.21, ...), kind=kOutput, calls=%fused_computation.73 | convolution fusion | flops 21641216 | bytes 5838080 | tf_op jit(solution)/shard_map/sub | solution.py:86
  130.2 0.4 convert_reduce_fusion
  130.6 4.0 %fusion.19 = bf16[8,4,80]{2,1,0:T(4,128)(2,1)S(1)} fusion(bf16[8,1,80,4096]{3,2,1,0:T(8,128)(2,1)} %param.16, bf16[8,4,4096]{2,1,0:T(4,128)(2,1)S(1)} %get-tuple-element.17, pred[8,4096]{1,0:T(8,128)(4,1)S(1)} %get-tuple-element.37, f32[8,80]{1,0:T(8,128)S(1)} %fusion.22, f32[8,4]{1,0:T(8,128)S(1)} %get-tuple-element.16), kind=kOutput, calls=%fused_computation.14 | convolution fusion | flops 21110272 | bytes 5545600 | tf_op jit(solution)/shard_map/rkgw,rkhw->rkgh/dot_general | solution.py:93
  135.3 0.5 broadcast.209
  135.9 0.7 reduce.7
  136.6 8.8 %all_to_all.5 = bf16[8,2,160]{2,1,0:T(2,128)(2,1)S(1)} all-to-all(bf16[8,2,160]{2,1,0:T(2,128)(2,1)S(1)} %reshape.327), channel_id=1, replica_groups=mesh['req'=32,'kv'=8] {'kv'}, dimensions={0} | all-to-all | bytes 10240 | tf_op jit(solution)/shard_map/all_to_all | solution.py:102
  145.6 0.7 reshape.315
  146.3 1.4 scatter_custom_fusion
  147.7 0.7 dynamic_slice.6
  150.3 98.7 %all-gather.7.cloned.1.call-done = bf16[256,1,2560]{2,1,0:T(2,128)(2,1)} async-done(((bf16[1,1,2560]{2,1,0:T(2,128)(2,1)}), bf16[256,1,2560]{2,1,0:T(2,128)(2,1)}) %all-gather.7.cloned.1.call-update) | async-done | bytes 1310736 | tf_op jit(solution)/shard_map/all_gather | solution.py:105
  249.0 1.3 fusion.29
  (38 shorter events, 1.6 us)
Async XLA Ops:
  6.5 119.0 %copy-start = (bf16[2560,320]{0,1:T(8,128)(2,1)S(1)}, bf16[2560,320]{0,1:T(8,128)(2,1)}, u32[]{:S(2)}) copy-start(bf16[2560,320]{0,1:T(8,128)(2,1)} %param.12) | copy-start | bytes 4915204
  6.5 113.6 %all-gather.5.cloned.1.call-start = ((), (), s32[]{:S(2)}) async-start(), calls=%async_computation.1 | async-start | bytes 2631680 | tf_op jit(solution)/shard_map/all_gather | solution.py:42
  7.3 241.8 %all-gather.7.cloned.1.call-start = ((), (), s32[]{:S(2)}) async-start(), calls=%async_computation.2 | async-start | bytes 2631680 | tf_op jit(solution)/shard_map/all_gather | solution.py:105
  126.5 19.8 %copy-start.1 = (s32[256]{0:T(256)S(1)}, s32[256]{0:T(256)}, u32[]{:S(2)}) copy-start(s32[256]{0:T(256)} %param.19) | copy-start | bytes 3076
Sparse Core Ops, SparseCore 0:
  11.0 109.0 all-gather.4
  146.4 102.5 all-gather.6
